TPU v7x, 512 devices: a whole 4x4x16 slice. The times are simulated.
512 devices in a mesh: wa: 32 (over x, y, core), ha: 16 (over z).
Axes of the slice: x: 4, y: 4, z: 16, core: 2. Of those that a mesh axis runs over, the one named last changes fastest.
Arguments:
- residual_in: bfloat16 [192, 16384], P('ha', 'wa'), may hold values from -43.25 to 43.25
- grad_out: bfloat16 [192, 16384], P('ha', 'wa'), may hold values from -6 to 6
- norm_gain: bfloat16 [16384], P('wa'), may hold values from 0.099609375 to 1.8984375
- w_gate: bfloat16 [16384, 26624], P('wa', 'ha'), may hold values from -0.0390625 to 0.0390625
- w_up: bfloat16 [16384, 26624], P('wa', 'ha'), may hold values from -0.0390625 to 0.0390625
- w_down: bfloat16 [26624, 16384], P('ha', 'wa'), may hold values from -0.030643146 to 0.030643146
Outputs:
- grad_in: bfloat16 [192, 16384], P('ha', 'wa')
All inputs are finite; a program needn't handle non-finite values.
Results may differ from a plain program's by a relative error of at most 0.0053.
Values may be sent and summed in bfloat16 or wider, within the bound.
No kernel may reach another device: no remote copies, remote signals or barrier semaphores. Data moves between devices by JAX's collectives and lax.ppermute only.
A program may use at most 64 MiB of HBM per device.

v0:
```python
import jax
import jax.numpy as jnp
from jax import lax
from jax.sharding import PartitionSpec as P

D = 16384


def gate_grads(gate, up, d_hidden):
    sig = jax.nn.sigmoid(gate)
    d_up = (d_hidden * gate * sig).astype(jnp.bfloat16)
    d_gate = (d_hidden * up * sig * (1.0 + gate * (1.0 - sig))).astype(jnp.bfloat16)
    return jnp.stack([d_gate, d_up])


def local(residual_in, grad_out, norm_gain, w_gate, w_up, w_down):
    stream = residual_in.astype(jnp.float32)
    squares = lax.psum(jnp.sum(stream * stream, axis=1), "wa")
    inv_rms = lax.rsqrt(squares / D + 1e-05)[:, None]
    gain_f = norm_gain.astype(jnp.float32)
    normed = (stream * inv_rms * gain_f).astype(jnp.bfloat16)
    stacked = jnp.stack([normed, grad_out])
    piece = lax.all_gather(stacked, "ha", axis=1, tiled=True)
    gate_part = jnp.dot(piece[0], w_gate, preferred_element_type=jnp.float32)
    up_part = jnp.dot(piece[0], w_up, preferred_element_type=jnp.float32)
    back_part = lax.dot_general(
        piece[1], w_down, (((1,), (1,)), ((), ())), preferred_element_type=jnp.float32
    )
    partial_sums = jnp.stack([gate_part, up_part, back_part])
    summed = lax.psum(partial_sums, "wa")
    grads = gate_grads(summed[0], summed[1], summed[2])
    total = lax.dot_general(
        grads[0], w_gate, (((1,), (1,)), ((), ())), preferred_element_type=jnp.float32
    )
    d_normed = lax.psum_scatter(
        total
        + lax.dot_general(
            grads[1], w_up, (((1,), (1,)), ((), ())), preferred_element_type=jnp.float32
        ),
        "ha",
        scatter_dimension=0,
        tiled=True,
    )
    scaled = d_normed * gain_f
    row_dot = lax.psum(jnp.sum(scaled * stream, axis=1), "wa")[:, None]
    grad_in = grad_out.astype(jnp.float32) + inv_rms * scaled - stream * inv_rms**3 * row_dot / D
    return grad_in.astype(jnp.bfloat16)


def solution(mesh):
    placed = (P("ha", "wa"), P("ha", "wa"), P("wa"), P("wa", "ha"), P("wa", "ha"), P("ha", "wa"))
    return jax.shard_map(
        local, mesh=mesh, in_specs=placed, out_specs=P("ha", "wa"), check_vma=False
    )
```

profile of v0, /device:TPU:1, one launch (start us, length us, event | category | flops | bytes accessed | tf_op | source)
XLA Modules:
  0.0 384.8 jit_solution(6059536915146214695)
XLA Ops:
  6.5 0.0 copy-start
  6.5 0.0 copy-start.2
  6.5 0.0 all-reduce.4.cloned.1.call-start
  6.5 1.0 fusion.8
  7.5 69.0 %psum.21 = f32[12]{0:T(128)S(1)} all-reduce(f32[12]{0:T(128)S(1)} %fusion.8), channel_id=1, replica_groups=mesh['wa'=32,'ha'=16] {'wa'}, use_global_device_ids=true, to_apply=%region_1.0 | all-reduce | flops 12 | bytes 96 | tf_op jit(solution)/shard_map/psum | solution.py:18
  76.5 0.7 convert_element_type.23
  77.2 0.8 fusion.16
  78.0 0.7 pad_maximum_fusion.1
  78.8 25.4 %all_gather.3 = bf16[2,192,512]{2,0,1:T(2,128)(2,1)S(1)} all-gather(bf16[2,12,512]{2,0,1:T(2,128)(2,1)S(1)} %copy.7), channel_id=1, replica_groups=mesh['wa'=32,'ha'=16] {'ha'}, dimensions={1}, use_global_device_ids=true | all-gather | bytes 417792 | tf_op jit(solution)/shard_map/all_gather | solution.py:23
  104.2 0.5 fusion.19
  104.7 0.0 copy-done.2
  104.7 0.5 convolution_bitcast_fusion.1
  105.3 0.0 copy-done
  105.3 0.0 copy-start.1
  105.3 0.5 convolution_bitcast_fusion.2
  105.8 0.9 copy-done.1
  106.7 0.7 convolution_bitcast_fusion
  107.4 2.1 pad_maximum_fusion
  109.6 0.0 all-reduce.4.cloned.1.call-update
  109.6 143.8 %all-reduce.4.cloned.1.call-done = f32[3,192,1664]{2,1,0:T(8,128)} async-done(((f32[3,192,1664]{2,1,0:T(8,128)}), f32[3,192,1664]{2,1,0:T(8,128)}) %all-reduce.4.cloned.1.call-update) | async-done | bytes 3833872 | tf_op jit(solution)/shard_map/psum | solution.py:30
  253.4 2.8 fusion.6
  256.2 0.0 copy-start.3
  256.2 0.0 copy-start.4
  256.2 3.2 convolution_add_fusion
  259.5 29.2 %fusion = f32[16,512]{1,0:T(8,128)S(1)} fusion(f32[192,512]{1,0:T(8,128)} %convolution_add_fusion), kind=kCustom, calls=%all-reduce-scatter | all-reduce-scatter fusion | flops 131073 | bytes 428032
  288.7 1.7 collective-permute-start
  290.4 2.7 collective-permute-start.1
  293.2 4.9 %collective-permute-start.2 = (f32[16,512]{1,0:T(8,128)S(1)}, f32[16,512]{1,0:T(8,128)S(1)}, u32[]{:S(2)}, u32[]{:S(2)}) collective-permute-start(f32[16,512]{1,0:T(8,128)S(1)} %fusion), channel_id=1, source_target_pairs={{0,3},{1,4},{2,5},{3,6},{4,7},{5,8},{6,9},{7,10},{8,11},{9,12},{10... | collective-permute-start | bytes 98312
  298.1 5.6 %collective-permute-start.3 = (f32[12,512]{1,0:T(8,128)S(1)}, f32[12,512]{1,0:T(8,128)S(1)}, u32[]{:S(2)}, u32[]{:S(2)}) collective-permute-start(f32[12,512]{1,0:T(8,128)S(1)} %slice.26), channel_id=1, source_target_pairs={{0,4},{1,5},{2,6},{3,7},{4,8},{5,9},{6,10},{7,11},{8,12},{9,13},{1... | collective-permute-start | bytes 73736
  303.7 1.3 dynamic-slice.4
  305.6 0.0 collective-permute-done.3
  305.6 0.0 collective-permute-done
  305.6 0.0 collective-permute-done.1
  305.6 0.0 collective-permute-done.2
  305.6 0.5 concatenate
  306.2 0.0 copy-done.3
  306.2 0.1 fusion.15
  306.3 71.0 %psum.23 = f32[12]{0:T(128)S(1)} all-reduce(f32[12]{0:T(128)S(1)} %fusion.15), channel_id=1, replica_groups=mesh['wa'=32,'ha'=16] {'wa'}, use_global_device_ids=true, to_apply=%region_5.0 | all-reduce | flops 12 | bytes 96 | tf_op jit(solution)/shard_map/psum | solution.py:45
  377.3 0.0 copy-done.4
  377.3 0.7 fusion.14
  (3 shorter events, 0.0 us)
Async XLA Ops:
  6.5 98.7 %copy-start = (bf16[512,1664]{1,0:T(8,128)(2,1)S(1)}, bf16[512,1664]{1,0:T(8,128)(2,1)}, u32[]{:S(2)}) copy-start(bf16[512,1664]{1,0:T(8,128)(2,1)} %param.9) | copy-start | bytes 5111812
  6.5 98.2 %copy-start.2 = (bf16[512,1664]{1,0:T(8,128)(2,1)S(1)}, bf16[512,1664]{1,0:T(8,128)(2,1)}, u32[]{:S(2)}) copy-start(bf16[512,1664]{1,0:T(8,128)(2,1)} %param.10) | copy-start | bytes 5111812
  6.5 246.9 %all-reduce.4.cloned.1.call-start = ((), (), s32[]{:S(2)}) async-start(), calls=%async_computation | async-start | bytes 7667712 | tf_op jit(solution)/shard_map/psum | solution.py:30
  105.3 1.5 copy-start.1
  256.2 50.0 %copy-start.3 = (bf16[12,512]{1,0:T(8,128)(2,1)S(1)}, bf16[12,512]{1,0:T(8,128)(2,1)}, u32[]{:S(2)}) copy-start(bf16[12,512]{1,0:T(8,128)(2,1)} %param.6) | copy-start | bytes 36868
  256.2 121.0 %copy-start.4 = (bf16[12,512]{1,0:T(8,128)(2,1)S(1)}, bf16[12,512]{1,0:T(8,128)(2,1)}, u32[]{:S(2)}) copy-start(bf16[12,512]{1,0:T(8,128)(2,1)} %param.7) | copy-start | bytes 36868
  288.7 16.9 %collective-permute-start = (f32[16,512]{1,0:T(8,128)S(1)}, f32[16,512]{1,0:T(8,128)S(1)}, u32[]{:S(2)}, u32[]{:S(2)}) collective-permute-start(f32[16,512]{1,0:T(8,128)S(1)} %fusion), channel_id=1, source_target_pairs={{0,1},{1,2},{2,3},{3,4},{4,5},{5,6},{6,7},{7,8},{8,9},{9,10},{10,1... | collective-permute-start | bytes 98312
  290.4 15.2 %collective-permute-start.1 = (f32[16,512]{1,0:T(8,128)S(1)}, f32[16,512]{1,0:T(8,128)S(1)}, u32[]{:S(2)}, u32[]{:S(2)}) collective-permute-start(f32[16,512]{1,0:T(8,128)S(1)} %fusion), channel_id=1, source_target_pairs={{0,2},{1,3},{2,4},{3,5},{4,6},{5,7},{6,8},{7,9},{8,10},{9,11},{10,... | collective-permute-start | bytes 98312
  293.2 12.5 %collective-permute-start.2 = (f32[16,512]{1,0:T(8,128)S(1)}, f32[16,512]{1,0:T(8,128)S(1)}, u32[]{:S(2)}, u32[]{:S(2)}) collective-permute-start(f32[16,512]{1,0:T(8,128)S(1)} %fusion), channel_id=1, source_target_pairs={{0,3},{1,4},{2,5},{3,6},{4,7},{5,8},{6,9},{7,10},{8,11},{9,12},{10... | collective-permute-start | bytes 98312
  298.1 7.5 %collective-permute-start.3 = (f32[12,512]{1,0:T(8,128)S(1)}, f32[12,512]{1,0:T(8,128)S(1)}, u32[]{:S(2)}, u32[]{:S(2)}) collective-permute-start(f32[12,512]{1,0:T(8,128)S(1)} %slice.26), channel_id=1, source_target_pairs={{0,4},{1,5},{2,6},{3,7},{4,8},{5,9},{6,10},{7,11},{8,12},{9,13},{1... | collective-permute-start | bytes 73736
Sparse Core Ops, SparseCore 0:
  109.7 143.6 all-reduce.3
where the time goes:
time: 385 us
  blocking collectives  195 us (51%)
  waiting for transfers between devices  144 us (37%)
  starting transfers between devices  14.9 us (4%)
  between operations  14.2 us (4%)
  matrix products  7.8 us (2%)
  other arithmetic  6.15 us (2%)
    psum x1, waiting for transfers between devices, local(): summed = lax.psum(partial_sums, 'wa')  144 us
    psum x1, blocking collectives, local(): row_dot = lax.psum(jnp.sum(scaled * stream, axis=1), 'wa')[:, None]  71 us
    psum x1, blocking collectives, local(): squares = lax.psum(jnp.sum(stream * stream, axis=1), 'wa')  69 us
    unnamed x1, blocking collectives  29.2 us
    all_gather x1, blocking collectives, local(): piece = lax.all_gather(stacked, 'ha', axis=1, tiled=True)  25.4 us
    unnamed x4, starting transfers between devices  14.9 us
  transfers between devices with their start and end apart: 5, of which 1 were waited for; matrix products, arithmetic and copies ran while one was open for 0% of the time, Pallas kernels for 0%

commit v1 on v0

--- a/solution.py
+++ b/solution.py
@@ -20,7 +20,24 @@
     gain_f = norm_gain.astype(jnp.float32)
     normed = (stream * inv_rms * gain_f).astype(jnp.bfloat16)
     stacked = jnp.stack([normed, grad_out])
-    piece = lax.all_gather(stacked, "ha", axis=1, tiled=True)
+    devices, position, rows = (lax.axis_size("ha"), lax.axis_index("ha"), stacked.shape[1])
+    right = [(i, (i + 1) % devices) for i in range(devices)]
+    backward = [(i, (i - 1) % devices) for i in range(devices)]
+    whole = jnp.zeros((*stacked.shape[:1], devices * rows, *stacked.shape[1 + 1 :]), stacked.dtype)
+    whole = lax.dynamic_update_slice_in_dim(whole, stacked, position * rows, axis=1)
+    from_left = from_right = stacked
+    half = devices // 2
+    for turn in range(1, half + 1):
+        from_left = lax.ppermute(from_left, "ha", right)
+        whole = lax.dynamic_update_slice_in_dim(
+            whole, from_left, (position - turn) % devices * rows, axis=1
+        )
+        if turn < devices - half:
+            from_right = lax.ppermute(from_right, "ha", backward)
+            whole = lax.dynamic_update_slice_in_dim(
+                whole, from_right, (position + turn) % devices * rows, axis=1
+            )
+    piece = whole
     gate_part = jnp.dot(piece[0], w_gate, preferred_element_type=jnp.float32)
     up_part = jnp.dot(piece[0], w_up, preferred_element_type=jnp.float32)
     back_part = lax.dot_general(

time: 385 us -> 414 us (1.075)
  starting transfers between devices: 14.9 us -> 64.2 us
  blocking collectives: 195 us -> 169 us
    ppermute x0 -> x15, starting transfers between devices: none -> 48.8 us  [the longest x7 33.5 us: local(): from_right = lax.ppermute(from_right, 'ha', backward)]
    all_gather x1 -> x0, blocking collectives: 25.4 us -> none  [local(): piece = lax.all_gather(stacked, 'ha', axis=1, tiled=True)]
  transfers between devices with their start and end apart: 5 -> 20, of which waited for: 1 -> 1; matrix products, arithmetic and copies ran while one was open for 0% -> 1% of each run, Pallas kernels for 0% -> 0%
where the time goes in v1:
time: 414 us; the launch traced here: 413 us
  blocking collectives  169 us (41%)
  waiting for transfers between devices  143 us (35%)
  starting transfers between devices  64.2 us (16%)
  between operations  15 us (4%)
  matrix products  9.35 us (2%)
  other arithmetic  6.11 us (1%)
  local copies, waits for them, and re-layouts  5.95 us (1%)
    psum x1, waiting for transfers between devices, local(): summed = lax.psum(partial_sums, 'wa')  143 us
    psum x1, blocking collectives, local(): row_dot = lax.psum(jnp.sum(scaled * stream, axis=1), 'wa')[:, None]  70.7 us
    psum x1, blocking collectives, local(): squares = lax.psum(jnp.sum(stream * stream, axis=1), 'wa')  68.9 us
    ppermute x7, starting transfers between devices, local(): from_right = lax.ppermute(from_right, 'ha', backward)  33.5 us
    unnamed x1, blocking collectives  29.3 us
    ppermute x8, starting transfers between devices, local(): from_left = lax.ppermute(from_left, 'ha', right)  15.4 us
    unnamed x4, starting transfers between devices  15.3 us
  transfers between devices with their start and end apart: 20, of which 1 were waited for; matrix products, arithmetic and copies ran while one was open for 1% of the time, Pallas kernels for 0%

profile of v1, /device:TPU:1, one launch (start us, length us, event | category | flops | bytes accessed | tf_op | source)
XLA Modules:
  0.0 412.8 jit_solution(1080212750354283671)
XLA Ops:
  6.5 1.0 fusion.8
  7.5 68.9 %psum.21 = f32[12]{0:T(128)S(1)} all-reduce(f32[12]{0:T(128)S(1)} %fusion.8), channel_id=1, replica_groups=mesh['wa'=32,'ha'=16] {'wa'}, use_global_device_ids=true, to_apply=%region_1.0 | all-reduce | flops 12 | bytes 96 | tf_op jit(solution)/shard_map/psum | solution.py:18
  76.4 0.7 convert_element_type.23
  77.1 0.8 fusion.16
  77.8 0.7 pad_maximum_fusion.1
  78.6 1.9 collective-permute-start
  80.5 6.0 %collective-permute-start.1 = (bf16[2,12,512]{2,1,0:T(8,128)(2,1)S(1)}, bf16[2,12,512]{2,1,0:T(8,128)(2,1)S(1)}, u32[]{:S(2)}, u32[]{:S(2)}) collective-permute-start(bf16[2,12,512]{2,1,0:T(8,128)(2,1)S(1)} %pad_maximum_fusion.1), channel_id=1, source_target_pairs={{0,15},{1,0},{2,1},{3,2},{4,3},{5,4},{6,5},{7,6},{8,7},{9,8},{10,9... | collective-permute-start | bytes 73736 | tf_op jit(solution)/shard_map/ppermute | solution.py:36
  86.5 1.9 collective-permute-start.2
  88.5 4.6 %collective-permute-start.3 = (bf16[2,12,512]{2,1,0:T(8,128)(2,1)S(1)}, bf16[2,12,512]{2,1,0:T(8,128)(2,1)S(1)}, u32[]{:S(2)}, u32[]{:S(2)}) collective-permute-start(bf16[2,12,512]{2,1,0:T(8,128)(2,1)S(1)} %collective-permute-done.1), channel_id=1, source_target_pairs={{0,15},{1,0},{2,1},{3,2},{4,3},{5,4},{6,5},{7,6},{8,7},{9,8},{10,9... | collective-permute-start | bytes 73736 | tf_op jit(solution)/shard_map/ppermute | solution.py:36
  93.1 1.9 collective-permute-start.4
  95.0 4.6 %collective-permute-start.5 = (bf16[2,12,512]{2,1,0:T(8,128)(2,1)S(1)}, bf16[2,12,512]{2,1,0:T(8,128)(2,1)S(1)}, u32[]{:S(2)}, u32[]{:S(2)}) collective-permute-start(bf16[2,12,512]{2,1,0:T(8,128)(2,1)S(1)} %collective-permute-done.3), channel_id=1, source_target_pairs={{0,15},{1,0},{2,1},{3,2},{4,3},{5,4},{6,5},{7,6},{8,7},{9,8},{10,9... | collective-permute-start | bytes 73736 | tf_op jit(solution)/shard_map/ppermute | solution.py:36
  99.6 1.9 collective-permute-start.6
  101.5 4.6 %collective-permute-start.7 = (bf16[2,12,512]{2,1,0:T(8,128)(2,1)S(1)}, bf16[2,12,512]{2,1,0:T(8,128)(2,1)S(1)}, u32[]{:S(2)}, u32[]{:S(2)}) collective-permute-start(bf16[2,12,512]{2,1,0:T(8,128)(2,1)S(1)} %collective-permute-done.5), channel_id=1, source_target_pairs={{0,15},{1,0},{2,1},{3,2},{4,3},{5,4},{6,5},{7,6},{8,7},{9,8},{10,9... | collective-permute-start | bytes 73736 | tf_op jit(solution)/shard_map/ppermute | solution.py:36
  106.1 1.9 collective-permute-start.8
  108.1 4.6 %collective-permute-start.9 = (bf16[2,12,512]{2,1,0:T(8,128)(2,1)S(1)}, bf16[2,12,512]{2,1,0:T(8,128)(2,1)S(1)}, u32[]{:S(2)}, u32[]{:S(2)}) collective-permute-start(bf16[2,12,512]{2,1,0:T(8,128)(2,1)S(1)} %collective-permute-done.7), channel_id=1, source_target_pairs={{0,15},{1,0},{2,1},{3,2},{4,3},{5,4},{6,5},{7,6},{8,7},{9,8},{10,9... | collective-permute-start | bytes 73736 | tf_op jit(solution)/shard_map/ppermute | solution.py:36
  112.7 1.9 collective-permute-start.10
  114.6 4.6 %collective-permute-start.11 = (bf16[2,12,512]{2,1,0:T(8,128)(2,1)S(1)}, bf16[2,12,512]{2,1,0:T(8,128)(2,1)S(1)}, u32[]{:S(2)}, u32[]{:S(2)}) collective-permute-start(bf16[2,12,512]{2,1,0:T(8,128)(2,1)S(1)} %collective-permute-done.9), channel_id=1, source_target_pairs={{0,15},{1,0},{2,1},{3,2},{4,3},{5,4},{6,5},{7,6},{8,7},{9,8},{10,9... | collective-permute-start | bytes 73736 | tf_op jit(solution)/shard_map/ppermute | solution.py:36
  119.2 1.9 collective-permute-start.12
  121.1 4.6 %collective-permute-start.13 = (bf16[2,12,512]{2,1,0:T(8,128)(2,1)S(1)}, bf16[2,12,512]{2,1,0:T(8,128)(2,1)S(1)}, u32[]{:S(2)}, u32[]{:S(2)}) collective-permute-start(bf16[2,12,512]{2,1,0:T(8,128)(2,1)S(1)} %collective-permute-done.11), channel_id=1, source_target_pairs={{0,15},{1,0},{2,1},{3,2},{4,3},{5,4},{6,5},{7,6},{8,7},{9,8},{10,9... | collective-permute-start | bytes 73736 | tf_op jit(solution)/shard_map/ppermute | solution.py:36
  125.7 1.9 collective-permute-start.14
  128.0 0.3 dynamic_update_slice.48
  128.5 0.3 dynamic_update_slice.50
  129.1 0.3 dynamic_update_slice.52
  129.3 0.3 dynamic_update_slice.53
  129.6 0.3 dynamic_update_slice.54
  129.9 0.3 dynamic_update_slice.55
  130.1 0.3 dynamic_update_slice.56
  130.4 0.3 dynamic_update_slice.57
  130.7 0.3 dynamic_update_slice.58
  130.9 0.3 dynamic_update_slice.59
  131.2 0.3 dynamic_update_slice.60
  131.5 0.3 dynamic_update_slice.61
  132.3 2.3 convolution_bitcast_fusion
  134.6 0.5 convolution_bitcast_fusion.1
  135.2 0.5 convolution_bitcast_fusion.2
  135.7 2.1 pad_maximum_fusion
  137.9 143.4 %all-reduce.4.cloned.1.call-done = f32[3,192,1664]{2,1,0:T(8,128)} async-done(((f32[3,192,1664]{2,1,0:T(8,128)}), f32[3,192,1664]{2,1,0:T(8,128)}) %all-reduce.4.cloned.1.call-update) | async-done | bytes 3833872 | tf_op jit(solution)/shard_map/psum | solution.py:47
  281.3 2.8 fusion.6
  284.1 3.2 convolution_add_fusion
  287.3 29.3 %fusion = f32[16,512]{1,0:T(8,128)S(1)} fusion(f32[192,512]{1,0:T(8,128)} %convolution_add_fusion), kind=kCustom, calls=%all-reduce-scatter | all-reduce-scatter fusion | flops 131073 | bytes 428032
  316.5 1.6 collective-permute-start.15
  318.1 2.9 collective-permute-start.16
  321.0 5.6 %collective-permute-start.17 = (f32[16,512]{1,0:T(8,128)S(1)}, f32[16,512]{1,0:T(8,128)S(1)}, u32[]{:S(2)}, u32[]{:S(2)}) collective-permute-start(f32[16,512]{1,0:T(8,128)S(1)} %fusion), channel_id=1, source_target_pairs={{0,3},{1,4},{2,5},{3,6},{4,7},{5,8},{6,9},{7,10},{8,11},{9,12},{10... | collective-permute-start | bytes 98312
  326.7 5.2 %collective-permute-start.18 = (f32[12,512]{1,0:T(8,128)S(1)}, f32[12,512]{1,0:T(8,128)S(1)}, u32[]{:S(2)}, u32[]{:S(2)}) collective-permute-start(f32[12,512]{1,0:T(8,128)S(1)} %slice.26), channel_id=1, source_target_pairs={{0,4},{1,5},{2,6},{3,7},{4,8},{5,9},{6,10},{7,11},{8,12},{9,13},{1... | collective-permute-start | bytes 73736
  331.9 1.3 dynamic-slice.4
  333.9 0.5 concatenate
  334.5 70.7 %psum.23 = f32[12]{0:T(128)S(1)} all-reduce(f32[12]{0:T(128)S(1)} %fusion.15), channel_id=1, replica_groups=mesh['wa'=32,'ha'=16] {'wa'}, use_global_device_ids=true, to_apply=%region_5.6 | all-reduce | flops 12 | bytes 96 | tf_op jit(solution)/shard_map/psum | solution.py:62
  405.2 0.7 fusion.14
  (39 shorter events, 1.2 us)
Async XLA Ops:
  6.5 128.6 %copy-start = (bf16[512,1664]{1,0:T(8,128)(2,1)S(1)}, bf16[512,1664]{1,0:T(8,128)(2,1)}, u32[]{:S(2)}) copy-start(bf16[512,1664]{1,0:T(8,128)(2,1)} %param.9) | copy-start | bytes 5111812
  6.5 274.7 %all-reduce.4.cloned.1.call-start = ((), (), s32[]{:S(2)}) async-start(), calls=%async_computation | async-start | bytes 7667712 | tf_op jit(solution)/shard_map/psum | solution.py:47
  78.6 8.0 %collective-permute-start = (bf16[2,12,512]{2,1,0:T(8,128)(2,1)S(1)}, bf16[2,12,512]{2,1,0:T(8,128)(2,1)S(1)}, u32[]{:S(2)}, u32[]{:S(2)}) collective-permute-start(bf16[2,12,512]{2,1,0:T(8,128)(2,1)S(1)} %pad_maximum_fusion.1), channel_id=1, source_target_pairs={{0,1},{1,2},{2,3},{3,4},{4,5},{5,6},{6,7},{7,8},{8,9},{9,10},{10,1... | collective-permute-start | bytes 73736 | tf_op jit(solution)/shard_map/ppermute | solution.py:31
  80.5 8.0 %collective-permute-start.1 = (bf16[2,12,512]{2,1,0:T(8,128)(2,1)S(1)}, bf16[2,12,512]{2,1,0:T(8,128)(2,1)S(1)}, u32[]{:S(2)}, u32[]{:S(2)}) collective-permute-start(bf16[2,12,512]{2,1,0:T(8,128)(2,1)S(1)} %pad_maximum_fusion.1), channel_id=1, source_target_pairs={{0,15},{1,0},{2,1},{3,2},{4,3},{5,4},{6,5},{7,6},{8,7},{9,8},{10,9... | collective-permute-start | bytes 73736 | tf_op jit(solution)/shard_map/ppermute | solution.py:36
  86.5 6.5 %collective-permute-start.2 = (bf16[2,12,512]{2,1,0:T(8,128)(2,1)S(1)}, bf16[2,12,512]{2,1,0:T(8,128)(2,1)S(1)}, u32[]{:S(2)}, u32[]{:S(2)}) collective-permute-start(bf16[2,12,512]{2,1,0:T(8,128)(2,1)S(1)} %collective-permute-done), channel_id=1, source_target_pairs={{0,1},{1,2},{2,3},{3,4},{4,5},{5,6},{6,7},{7,8},{8,9},{9,10},{10,1... | collective-permute-start | bytes 73736 | tf_op jit(solution)/shard_map/ppermute | solution.py:31
  88.5 6.5 %collective-permute-start.3 = (bf16[2,12,512]{2,1,0:T(8,128)(2,1)S(1)}, bf16[2,12,512]{2,1,0:T(8,128)(2,1)S(1)}, u32[]{:S(2)}, u32[]{:S(2)}) collective-permute-start(bf16[2,12,512]{2,1,0:T(8,128)(2,1)S(1)} %collective-permute-done.1), channel_id=1, source_target_pairs={{0,15},{1,0},{2,1},{3,2},{4,3},{5,4},{6,5},{7,6},{8,7},{9,8},{10,9... | collective-permute-start | bytes 73736 | tf_op jit(solution)/shard_map/ppermute | solution.py:36
  93.1 6.5 %collective-permute-start.4 = (bf16[2,12,512]{2,1,0:T(8,128)(2,1)S(1)}, bf16[2,12,512]{2,1,0:T(8,128)(2,1)S(1)}, u32[]{:S(2)}, u32[]{:S(2)}) collective-permute-start(bf16[2,12,512]{2,1,0:T(8,128)(2,1)S(1)} %collective-permute-done.2), channel_id=1, source_target_pairs={{0,1},{1,2},{2,3},{3,4},{4,5},{5,6},{6,7},{7,8},{8,9},{9,10},{10,1... | collective-permute-start | bytes 73736 | tf_op jit(solution)/shard_map/ppermute | solution.py:31
  95.0 6.5 %collective-permute-start.5 = (bf16[2,12,512]{2,1,0:T(8,128)(2,1)S(1)}, bf16[2,12,512]{2,1,0:T(8,128)(2,1)S(1)}, u32[]{:S(2)}, u32[]{:S(2)}) collective-permute-start(bf16[2,12,512]{2,1,0:T(8,128)(2,1)S(1)} %collective-permute-done.3), channel_id=1, source_target_pairs={{0,15},{1,0},{2,1},{3,2},{4,3},{5,4},{6,5},{7,6},{8,7},{9,8},{10,9... | collective-permute-start | bytes 73736 | tf_op jit(solution)/shard_map/ppermute | solution.py:36
  99.6 6.5 %collective-permute-start.6 = (bf16[2,12,512]{2,1,0:T(8,128)(2,1)S(1)}, bf16[2,12,512]{2,1,0:T(8,128)(2,1)S(1)}, u32[]{:S(2)}, u32[]{:S(2)}) collective-permute-start(bf16[2,12,512]{2,1,0:T(8,128)(2,1)S(1)} %collective-permute-done.4), channel_id=1, source_target_pairs={{0,1},{1,2},{2,3},{3,4},{4,5},{5,6},{6,7},{7,8},{8,9},{9,10},{10,1... | collective-permute-start | bytes 73736 | tf_op jit(solution)/shard_map/ppermute | solution.py:31
  101.5 6.5 %collective-permute-start.7 = (bf16[2,12,512]{2,1,0:T(8,128)(2,1)S(1)}, bf16[2,12,512]{2,1,0:T(8,128)(2,1)S(1)}, u32[]{:S(2)}, u32[]{:S(2)}) collective-permute-start(bf16[2,12,512]{2,1,0:T(8,128)(2,1)S(1)} %collective-permute-done.5), channel_id=1, source_target_pairs={{0,15},{1,0},{2,1},{3,2},{4,3},{5,4},{6,5},{7,6},{8,7},{9,8},{10,9... | collective-permute-start | bytes 73736 | tf_op jit(solution)/shard_map/ppermute | solution.py:36
  106.1 6.5 %collective-permute-start.8 = (bf16[2,12,512]{2,1,0:T(8,128)(2,1)S(1)}, bf16[2,12,512]{2,1,0:T(8,128)(2,1)S(1)}, u32[]{:S(2)}, u32[]{:S(2)}) collective-permute-start(bf16[2,12,512]{2,1,0:T(8,128)(2,1)S(1)} %collective-permute-done.6), channel_id=1, source_target_pairs={{0,1},{1,2},{2,3},{3,4},{4,5},{5,6},{6,7},{7,8},{8,9},{9,10},{10,1... | collective-permute-start | bytes 73736 | tf_op jit(solution)/shard_map/ppermute | solution.py:31
  108.1 6.5 %collective-permute-start.9 = (bf16[2,12,512]{2,1,0:T(8,128)(2,1)S(1)}, bf16[2,12,512]{2,1,0:T(8,128)(2,1)S(1)}, u32[]{:S(2)}, u32[]{:S(2)}) collective-permute-start(bf16[2,12,512]{2,1,0:T(8,128)(2,1)S(1)} %collective-permute-done.7), channel_id=1, source_target_pairs={{0,15},{1,0},{2,1},{3,2},{4,3},{5,4},{6,5},{7,6},{8,7},{9,8},{10,9... | collective-permute-start | bytes 73736 | tf_op jit(solution)/shard_map/ppermute | solution.py:36
  112.7 6.5 %collective-permute-start.10 = (bf16[2,12,512]{2,1,0:T(8,128)(2,1)S(1)}, bf16[2,12,512]{2,1,0:T(8,128)(2,1)S(1)}, u32[]{:S(2)}, u32[]{:S(2)}) collective-permute-start(bf16[2,12,512]{2,1,0:T(8,128)(2,1)S(1)} %collective-permute-done.8), channel_id=1, source_target_pairs={{0,1},{1,2},{2,3},{3,4},{4,5},{5,6},{6,7},{7,8},{8,9},{9,10},{10,1... | collective-permute-start | bytes 73736 | tf_op jit(solution)/shard_map/ppermute | solution.py:31
  114.6 6.5 %collective-permute-start.11 = (bf16[2,12,512]{2,1,0:T(8,128)(2,1)S(1)}, bf16[2,12,512]{2,1,0:T(8,128)(2,1)S(1)}, u32[]{:S(2)}, u32[]{:S(2)}) collective-permute-start(bf16[2,12,512]{2,1,0:T(8,128)(2,1)S(1)} %collective-permute-done.9), channel_id=1, source_target_pairs={{0,15},{1,0},{2,1},{3,2},{4,3},{5,4},{6,5},{7,6},{8,7},{9,8},{10,9... | collective-permute-start | bytes 73736 | tf_op jit(solution)/shard_map/ppermute | solution.py:36
  119.2 6.5 %collective-permute-start.12 = (bf16[2,12,512]{2,1,0:T(8,128)(2,1)S(1)}, bf16[2,12,512]{2,1,0:T(8,128)(2,1)S(1)}, u32[]{:S(2)}, u32[]{:S(2)}) collective-permute-start(bf16[2,12,512]{2,1,0:T(8,128)(2,1)S(1)} %collective-permute-done.10), channel_id=1, source_target_pairs={{0,1},{1,2},{2,3},{3,4},{4,5},{5,6},{6,7},{7,8},{8,9},{9,10},{10,1... | collective-permute-start | bytes 73736 | tf_op jit(solution)/shard_map/ppermute | solution.py:31
  121.1 10.6 %collective-permute-start.13 = (bf16[2,12,512]{2,1,0:T(8,128)(2,1)S(1)}, bf16[2,12,512]{2,1,0:T(8,128)(2,1)S(1)}, u32[]{:S(2)}, u32[]{:S(2)}) collective-permute-start(bf16[2,12,512]{2,1,0:T(8,128)(2,1)S(1)} %collective-permute-done.11), channel_id=1, source_target_pairs={{0,15},{1,0},{2,1},{3,2},{4,3},{5,4},{6,5},{7,6},{8,7},{9,8},{10,9... | collective-permute-start | bytes 73736 | tf_op jit(solution)/shard_map/ppermute | solution.py:36
  125.7 6.3 %collective-permute-start.14 = (bf16[2,12,512]{2,1,0:T(8,128)(2,1)S(1)}, bf16[2,12,512]{2,1,0:T(8,128)(2,1)S(1)}, u32[]{:S(2)}, u32[]{:S(2)}) collective-permute-start(bf16[2,12,512]{2,1,0:T(8,128)(2,1)S(1)} %collective-permute-done.12), channel_id=1, source_target_pairs={{0,1},{1,2},{2,3},{3,4},{4,5},{5,6},{6,7},{7,8},{8,9},{9,10},{10,1... | collective-permute-start | bytes 73736 | tf_op jit(solution)/shard_map/ppermute | solution.py:31
  132.3 2.3 copy-start.1
  137.9 146.2 %copy-start.2 = (bf16[512,1664]{1,0:T(8,128)(2,1)S(1)}, bf16[512,1664]{1,0:T(8,128)(2,1)}, u32[]{:S(2)}) copy-start(bf16[512,1664]{1,0:T(8,128)(2,1)} %param.10) | copy-start | bytes 5111812
  284.1 50.3 %copy-start.3 = (bf16[12,512]{1,0:T(8,128)(2,1)S(1)}, bf16[12,512]{1,0:T(8,128)(2,1)}, u32[]{:S(2)}) copy-start(bf16[12,512]{1,0:T(8,128)(2,1)} %param.6) | copy-start | bytes 36868
  284.1 121.2 %copy-start.4 = (bf16[12,512]{1,0:T(8,128)(2,1)S(1)}, bf16[12,512]{1,0:T(8,128)(2,1)}, u32[]{:S(2)}) copy-start(bf16[12,512]{1,0:T(8,128)(2,1)} %param.7) | copy-start | bytes 36868
  316.5 17.3 %collective-permute-start.15 = (f32[16,512]{1,0:T(8,128)S(1)}, f32[16,512]{1,0:T(8,128)S(1)}, u32[]{:S(2)}, u32[]{:S(2)}) collective-permute-start(f32[16,512]{1,0:T(8,128)S(1)} %fusion), channel_id=1, source_target_pairs={{0,1},{1,2},{2,3},{3,4},{4,5},{5,6},{6,7},{7,8},{8,9},{9,10},{10,1... | collective-permute-start | bytes 98312
  318.1 15.7 %collective-permute-start.16 = (f32[16,512]{1,0:T(8,128)S(1)}, f32[16,512]{1,0:T(8,128)S(1)}, u32[]{:S(2)}, u32[]{:S(2)}) collective-permute-start(f32[16,512]{1,0:T(8,128)S(1)} %fusion), channel_id=1, source_target_pairs={{0,2},{1,3},{2,4},{3,5},{4,6},{5,7},{6,8},{7,9},{8,10},{9,11},{10,... | collective-permute-start | bytes 98312
  321.0 12.8 %collective-permute-start.17 = (f32[16,512]{1,0:T(8,128)S(1)}, f32[16,512]{1,0:T(8,128)S(1)}, u32[]{:S(2)}, u32[]{:S(2)}) collective-permute-start(f32[16,512]{1,0:T(8,128)S(1)} %fusion), channel_id=1, source_target_pairs={{0,3},{1,4},{2,5},{3,6},{4,7},{5,8},{6,9},{7,10},{8,11},{9,12},{10... | collective-permute-start | bytes 98312
  326.7 7.2 %collective-permute-start.18 = (f32[12,512]{1,0:T(8,128)S(1)}, f32[12,512]{1,0:T(8,128)S(1)}, u32[]{:S(2)}, u32[]{:S(2)}) collective-permute-start(f32[12,512]{1,0:T(8,128)S(1)} %slice.26), channel_id=1, source_target_pairs={{0,4},{1,5},{2,6},{3,7},{4,8},{5,9},{6,10},{7,11},{8,12},{9,13},{1... | collective-permute-start | bytes 73736
Sparse Core Ops, SparseCore 0:
  138.0 143.2 all-reduce.3
